TPU v7x, 256 devices: a whole 4x4x8 slice. The times are simulated.
256 devices in a mesh: fsdp: 16 (over x, y), seq: 16 (over z, core).
Axes of the slice: x: 4, y: 4, z: 8, core: 2. Of those that a mesh axis runs over, the one named last changes fastest.
Arguments:
- tokens: bfloat16 [65536, 2048], P(('fsdp', 'seq')), may hold values from -6 to 6
- seq_lengths: int32 [16, 4], P('fsdp'), may hold values from 1 to 2048, 4096 in all within a row
- in_weight: bfloat16 [2048, 6144], P(None, 'fsdp'), may hold values from -0.125 to 0.125
- short_filter: float32 [7, 6144], replicated, may hold values from -2.5 to 2.5
- long_filter: bfloat16 [128, 128], replicated, may hold values from -0.5 to 0.5
- out_weight: bfloat16 [2048, 2048], replicated, may hold values from -0.125 to 0.125
Outputs:
- mixed: bfloat16 [65536, 2048], P(('fsdp', 'seq'))
Inputs may be any that keep to these rules, and one draw needn't show every extreme that they name: `seq_lengths`: in each pack the 4 lengths sum to 4096 and the longest is exactly 2048.
All inputs are finite; a program needn't handle non-finite values.
Results may differ from a plain program's by a relative error of at most 0.0073.
Values may be sent and summed in bfloat16 or wider, within the bound.
No kernel may reach another device: no remote copies, remote signals or barrier semaphores. Data moves between devices by JAX's collectives and lax.ppermute only.
A program may use at most 128 MiB of HBM per device.

v0:
```python
import jax
import jax.numpy as jnp
from jax import lax
from jax.sharding import PartitionSpec as P

LANE = 128
GROUP_DEVS = 4


def positions(row_ids, seq_starts):
    seq_begin = jnp.max(
        jnp.where(seq_starts[None, :] <= row_ids[:, None], seq_starts[None, :], 0), axis=1
    )
    return row_ids - seq_begin


def tap_table(tap_ids, long_filter):
    filter_len = long_filter.shape[0]
    one_hot = (
        tap_ids[:, :, None] == jnp.arange(filter_len, dtype=jnp.int32)[None, None, :]
    ).astype(jnp.bfloat16)
    return jnp.einsum(
        "ijt,tg->gij", one_hot, long_filter, preferred_element_type=jnp.float32
    ).astype(jnp.bfloat16)


def local(tokens, seq_lengths, in_weight, short_filter, long_filter, out_weight):
    rows, channels = tokens.shape
    width = short_filter.shape[0]
    filter_len, group_count = long_filter.shape
    per_group = channels // group_count
    n_seq = lax.axis_size("seq")
    s = lax.axis_index("seq")
    member = s % GROUP_DEVS
    part = LANE // GROUP_DEVS
    n_lblk = channels // LANE
    tail = filter_len + 8
    span = GROUP_DEVS * rows
    ext_rows = tail + span
    swaps = [[(i, i ^ d) for i in range(n_seq)] for d in range(1, GROUP_DEVS)]
    from_member = [tokens, lax.ppermute(tokens, "seq", swaps[0])]
    for d in range(2, GROUP_DEVS, 2):
        fetched = lax.ppermute(tokens, "seq", swaps[d - 1])
        from_member += [fetched, lax.ppermute(fetched, "seq", swaps[0])]
    blocks = []
    for m in range(GROUP_DEVS):
        pick = from_member[0]
        for d in range(1, GROUP_DEVS):
            pick = jnp.where(member ^ d == m, from_member[d], pick)
        blocks.append(pick)
    tail_src = tokens[rows - tail :]
    tail_tok = jnp.zeros_like(tail_src)
    for m in range(GROUP_DEVS):
        dist = m + 1
        perm = [(i - dist, i) for i in range(GROUP_DEVS, n_seq) if i % GROUP_DEVS == m]
        got = lax.ppermute(tail_src, "seq", perm)
        tail_tok = jnp.where(member == m, got, tail_tok)
    ext_tokens = jnp.concatenate([tail_tok] + blocks, axis=0)
    lengths_row = seq_lengths[0]
    seq_starts = jnp.cumsum(lengths_row) - lengths_row
    pair_start = s // GROUP_DEVS * span
    row_ids = pair_start - tail + jnp.arange(ext_rows, dtype=jnp.int32)
    position = positions(row_ids, seq_starts)
    offset = member * part
    w_t = in_weight.T.reshape(in_weight.shape[1] // LANE, LANE, channels)
    w_part = lax.dynamic_slice_in_dim(w_t, offset, part, axis=1)
    w_all = lax.all_gather(w_part, "fsdp", axis=0, tiled=True)
    own = n_lblk * part
    w_all = w_all.reshape(3 * own, channels)
    ow = out_weight.reshape(n_lblk, LANE, channels)
    weights = []
    for d in range(GROUP_DEVS):
        src_offset = (member ^ d) * part
        weights.append(
            lax.dynamic_slice_in_dim(ow, src_offset, part, axis=1).reshape(own, channels)
        )
    ow_cat = jnp.concatenate(weights, axis=0)
    ext_tokens, ow_cat = lax.optimization_barrier((ext_tokens, ow_cat))
    projected = jnp.dot(ext_tokens, w_all.T, preferred_element_type=jnp.float32).astype(
        jnp.bfloat16
    )
    taps = short_filter.reshape(width, 3, n_lblk, LANE)
    taps = lax.dynamic_slice_in_dim(taps, offset, part, axis=3).reshape(width, 3 * own)
    start = 8
    feat_rows = ext_rows - start
    pos_f = position[start:]
    featured = jnp.zeros((feat_rows, 3 * own), jnp.float32)
    for tap_index in range(width):
        shifted = projected[start - tap_index : ext_rows - tap_index].astype(jnp.float32)
        featured = featured + taps[tap_index] * jnp.where(
            (pos_f >= tap_index)[:, None], shifted, 0.0
        )
    queries = featured[feat_rows - span :, :own]
    mixed_in = (featured[:, own : 2 * own] * featured[:, 2 * own :]).astype(jnp.bfloat16)
    sub = LANE // per_group
    lf = long_filter.reshape(filter_len, n_lblk, sub)
    lf = lax.dynamic_slice_in_dim(lf, offset // per_group, part // per_group, axis=2)
    lf = lf.reshape(filter_len, own // per_group)
    n_groups = own // per_group
    out_rows = jnp.arange(filter_len, dtype=jnp.int32)[:, None]
    src_rows = jnp.arange(filter_len, dtype=jnp.int32)[None, :]
    cur_tap = out_rows - src_rows
    prev_tap = out_rows + filter_len - src_rows
    cur_table = tap_table(cur_tap, lf)
    prev_table = tap_table(prev_tap, lf)
    n_blocks = span // filter_len
    pos_out = position[tail:].reshape(n_blocks, filter_len)
    cur_kernel = jnp.where(
        (cur_tap[None] <= pos_out[:, :, None])[:, None], cur_table[None], 0.0
    ).astype(jnp.bfloat16)
    prev_kernel = jnp.where(
        (prev_tap[None] <= pos_out[:, :, None])[:, None], prev_table[None], 0.0
    ).astype(jnp.bfloat16)
    mi_t = mixed_in.T.reshape(n_groups, per_group, n_blocks + 1, filter_len)
    filtered = jnp.einsum(
        "gcbj,bgij->gcbi", mi_t[:, :, 1:], cur_kernel, preferred_element_type=jnp.float32
    )
    filtered = filtered + jnp.einsum(
        "gcbj,bgij->gcbi", mi_t[:, :, :-1], prev_kernel, preferred_element_type=jnp.float32
    )
    filtered = filtered.reshape(own, span)
    gated = (queries.T * filtered).astype(jnp.bfloat16)
    gated = gated.T.reshape(GROUP_DEVS, rows, own)
    pieces = []
    for d in range(GROUP_DEVS):
        send = lax.dynamic_index_in_dim(gated, member ^ d, axis=0, keepdims=False)
        got = send if d == 0 else lax.ppermute(send, "seq", swaps[d - 1])
        pieces.append(got)
    result = tokens.astype(jnp.float32) + jnp.dot(
        jnp.concatenate(pieces, axis=1), ow_cat, preferred_element_type=jnp.float32
    )
    return result.astype(jnp.bfloat16)


def solution(mesh):
    in_specs = (P(("fsdp", "seq"), None), P("fsdp", None), P(None, "fsdp"), P(), P(), P())
    out_specs = P(("fsdp", "seq"), None)
    return jax.shard_map(local, mesh=mesh, in_specs=in_specs, out_specs=out_specs, check_vma=False)
```

profile of v0, /device:TPU:1, one launch (start us, length us, event | category | flops | bytes accessed | tf_op | source)
XLA Modules:
  0.0 154.7 jit_solution(10799367417863991124)
XLA Ops:
  6.5 1.8 %copy.26 = bf16[2048,384]{0,1:T(8,128)(2,1)S(1)} copy(bf16[2048,384]{1,0:T(8,128)(2,1)} %param.8) | data formatting | bytes 3145728 | tf_op args[2]
  15.4 8.6 %collective-permute-start.4 = (bf16[256,2048]{1,0:T(8,128)(2,1)S(1)}, bf16[256,2048]{1,0:T(8,128)(2,1)S(1)}, u32[]{:S(2)}, u32[]{:S(2)}) collective-permute-start(bf16[256,2048]{1,0:T(8,128)(2,1)S(1)} %copy-done.1), channel_id=1, source_target_pairs={{0,2},{1,3},{2,0},{3,1},{4,6},{5,7},{6,4},{7,5},{8,10},{9,11},{10,... | collective-permute-start | bytes 3145736 | tf_op jit(solution)/shard_map/ppermute | solution.py:43
  27.4 4.0 %fusion.20 = bf16[32,128,128]{2,0,1:T(8,128)(2,1)S(1)} fusion(bf16[128,32,1]{0,1,2:T(8,128)(2,1)S(1)} %bitcast.77, s32[128,128]{1,0:T(8,128)S(1)} %get-tuple-element.35), kind=kOutput, calls=%fused_computation.28 | convolution fusion | flops 136839168 | bytes 1122304 | tf_op jit(solution)/shard_map/ijt,tg->gij/dot_general | solution.py:22
  32.8 3.9 %fusion.21 = bf16[32,128,128]{2,0,1:T(8,128)(2,1)S(1)} fusion(bf16[128,32,1]{0,1,2:T(8,128)(2,1)S(1)} %bitcast.78, s32[128,128]{1,0:T(8,128)S(1)} %get-tuple-element.36), kind=kOutput, calls=%fused_computation.29 | convolution fusion | flops 136839168 | bytes 1122304 | tf_op jit(solution)/shard_map/ijt,tg->gij/dot_general | solution.py:22
  39.2 4.3 %constant_dynamic-slice_fusion.11 = (bf16[16,32,2048]{2,1,0:T(8,128)(2,1)S(1)}, bf16[16,32,2048]{2,1,0:T(8,128)(2,1)S(1)}, bf16[16,32,2048]{2,1,0:T(8,128)(2,1)S(1)}, bf16[16,32,2048]{2,1,0:T(8,128)(2,1)S(1)}) fusion(bf16[16,128,2048]{2,1,0:T(8,128)(2,1)} %bitcast.65, s32[]{:T(128)S(6)} %select_n.178, s32[]{:T(128)S(6)} %select_n.215, s32[]{:T(128)S(6)} %select_n.214, ...), kind=kLoop, calls=%fused_computation.73 | loop fusion | bytes 16777232 | tf_op jit(solution)/shard_map/dynamic_slice | solution.py:75
  44.2 4.1 %pad_maximum_fusion = bf16[2048,2048]{1,0:T(8,128)(2,1)} fusion(bf16[512,2048]{1,0:T(8,128)(2,1)S(1)} %bitcast.69, bf16[512,2048]{1,0:T(8,128)(2,1)S(1)} %bitcast.70, bf16[512,2048]{1,0:T(8,128)(2,1)S(1)} %bitcast.71, bf16[512,2048]{1,0:T(8,128)(2,1)S(1)} %bitcast.68), kind=kLoop, calls=%fused_computation | loop fusion | flops 33554432 | bytes 16777216 | tf_op jit(solution)/shard_map/concatenate | solution.py:77
  48.3 2.3 %select_dynamic-update-slice_fusion.4 = bf16[1160,2048]{1,0:T(8,128)(2,1)} fusion(bf16[136,2048]{1,0:T(8,128)(2,1)S(1)} %collective-permute-done, bf16[136,2048]{1,0:T(8,128)(2,1)} %collective-permute-done.1, bf16[136,2048]{1,0:T(8,128)(2,1)} %collective-permute-done.2, bf16[136,2048]{1,0:T(8,128)(2,1)} %collective-permute-done.3, pred[]{:T(512)S(6)} %eq.79, ...), kind=kLoop, calls=%fused_computation.44 | loop fusion | flops 1114111 | bytes 2785284
  50.6 1.7 %select_dynamic-update-slice_fusion.3 = bf16[1160,2048]{1,0:T(8,128)(2,1)} fusion(bf16[1160,2048]{1,0:T(8,128)(2,1)} %select_dynamic-update-slice_fusion.4, bf16[256,2048]{1,0:T(8,128)(2,1)S(1)} %collective-permute-done.5, bf16[256,2048]{1,0:T(8,128)(2,1)S(1)} %collective-permute-done.4, bf16[256,2048]{1,0:T(8,128)(2,1)S(1)} %collective-permute-done.6, ...), kind=kLoop, calls=%fused_computation.43 | loop fusion | flops 1572864 | bytes 5242883
  52.3 1.7 %select_dynamic-update-slice_fusion.2 = bf16[1160,2048]{1,0:T(8,128)(2,1)} fusion(bf16[1160,2048]{1,0:T(8,128)(2,1)} %select_dynamic-update-slice_fusion.3, bf16[256,2048]{1,0:T(8,128)(2,1)S(1)} %collective-permute-done.5, bf16[256,2048]{1,0:T(8,128)(2,1)S(1)} %collective-permute-done.4, bf16[256,2048]{1,0:T(8,128)(2,1)S(1)} %collective-permute-done.6, ...), kind=kLoop, calls=%fused_computation.42 | loop fusion | flops 1572864 | bytes 5242883
  54.0 1.7 %select_dynamic-update-slice_fusion.1 = bf16[1160,2048]{1,0:T(8,128)(2,1)} fusion(bf16[1160,2048]{1,0:T(8,128)(2,1)} %select_dynamic-update-slice_fusion.2, bf16[256,2048]{1,0:T(8,128)(2,1)S(1)} %collective-permute-done.5, bf16[256,2048]{1,0:T(8,128)(2,1)S(1)} %collective-permute-done.4, bf16[256,2048]{1,0:T(8,128)(2,1)S(1)} %collective-permute-done.6, ...), kind=kLoop, calls=%fused_computation.41 | loop fusion | flops 1572864 | bytes 5242883
  55.7 1.7 %select_dynamic-update-slice_fusion = bf16[1160,2048]{1,0:T(8,128)(2,1)} fusion(bf16[1160,2048]{1,0:T(8,128)(2,1)} %select_dynamic-update-slice_fusion.1, bf16[256,2048]{1,0:T(8,128)(2,1)S(1)} %collective-permute-done.5, bf16[256,2048]{1,0:T(8,128)(2,1)S(1)} %collective-permute-done.4, bf16[256,2048]{1,0:T(8,128)(2,1)S(1)} %collective-permute-done.6, ...), kind=kLoop, calls=%fused_computation.40 | loop fusion | flops 1572864 | bytes 5242883 | tf_op jit(solution)/shard_map/concatenate | solution.py:58
  57.4 22.7 %all-gather.2.cloned.1.call-done = bf16[48,32,2048]{2,1,0:T(8,128)(2,1)} async-done(((bf16[3,32,2048]{2,1,0:T(8,128)(2,1)}), bf16[48,32,2048]{2,1,0:T(8,128)(2,1)}) %all-gather.2.cloned.1.call-update) | async-done | bytes 6291472 | tf_op jit(solution)/shard_map/all_gather | solution.py:67
  80.1 11.2 %convolution_convert_fusion = bf16[1160,1536]{1,0:T(8,128)(2,1)S(1)} fusion(bf16[1160,2048]{1,0:T(8,128)(2,1)} %select_dynamic-update-slice_fusion, bf16[1536,2048]{1,0:T(8,128)(2,1)} %bitcast.79), kind=kOutput, calls=%fused_computation.11 | convolution fusion | flops 7299870720 | bytes 14606336 | tf_op jit(solution)/shard_map/dot_general | solution.py:79
  91.2 10.7 %multiply_add_fusion = f32[1152,1536]{1,0:T(8,128)S(1)} fusion(bf16[1160,1536]{1,0:T(8,128)(2,1)S(1)} %convolution_convert_fusion, f32[1536]{0:T(1024)S(1)} %mul.115, f32[1536]{0:T(1024)S(1)} %mul.112, f32[1536]{0:T(1024)S(1)} %mul.109, f32[1536]{0:T(1024)S(1)} %mul.106, f32[1536]{0:T(1024)S(1)} %mul.103, f32[1536]{0:T(1024)S(1)} %mul.100, ...), kind=kLoop, calls=%fused_computation.12 | loop fusion | flops 47775744 | bytes 31901568 | tf_op jit(solution)/shard_map/add | solution.py:90
  101.9 2.9 %copy-done = f32[1152,1536]{1,0:T(8,128)} copy-done((f32[1152,1536]{1,0:T(8,128)}, f32[1152,1536]{1,0:T(8,128)S(1)}, u32[]{:S(2)}) %copy-start) | copy-done | bytes 7077912
  106.7 2.7 %reshape.154 = bf16[32,16,9,128]{3,2,1,0:T(8,128)(2,1)S(1)} reshape(bf16[512,1152]{1,0:T(8,128)(2,1)} %copy.29) | data formatting | bytes 2359296 | tf_op jit(solution)/shard_map/reshape | solution.py:114
  109.9 5.8 %fusion = f32[32,8,128,16]{2,3,1,0:T(8,128)S(1)} fusion(pred[8,128,128]{2,1,0:T(8,128)(4,1)S(1)} %copy-done.3, bf16[32,128,128]{2,1,0:T(8,128)(2,1)} %copy.31, bf16[32,16,8,128]{3,2,1,0:T(8,128)(2,1)S(1)} %get-tuple-element.14), kind=kOutput, calls=%fused_computation.1 | convolution fusion | flops 138412032 | bytes 4325376 | tf_op jit(solution)/shard_map/gcbj,bgij->gcbi/dot_general | solution.py:118
  115.6 4.5 %add_bitcast_fusion = f32[32,16,8,128]{3,1,2,0:T(8,128)S(1)} fusion(f32[32,8,128,16]{2,3,1,0:T(8,128)S(1)} %fusion, pred[8,128,128]{2,1,0:T(8,128)(4,1)S(1)} %get-tuple-element.33, bf16[32,128,128]{2,1,0:T(8,128)(2,1)S(1)} %copy-done.2, bf16[32,16,8,128]{3,2,1,0:T(8,128)(2,1)S(1)} %get-tuple-element.13), kind=kOutput, calls=%fused_computation.27 | convolution fusion | flops 138936320 | bytes 6422528 | tf_op jit(solution)/shard_map/gcbj,bgij->gcbi/dot_general | solution.py:115
  121.0 1.8 %copy.44 = f32[64,8,8,128]{3,1,2,0:T(8,128)} copy(f32[64,8,8,128]{3,2,1,0:T(8,128)S(1)} %bitcast.66) | data formatting | bytes 4194304
  122.8 1.9 %copy.34 = f32[512,1024]{0,1:T(8,128)S(1)} copy(f32[512,1024]{1,0:T(8,128)} %bitcast.67) | data formatting | bytes 4194304 | tf_op jit(solution)/shard_map/reshape | solution.py:121
  124.7 1.9 %fusion.17 = bf16[512,1024]{0,1:T(8,128)(2,1)S(1)} fusion(f32[512,1024]{0,1:T(8,128)S(1)} %copy.34, f32[1152,1536]{1,0:T(8,128)} %copy-done), kind=kLoop, calls=%fused_computation.26 | loop fusion | flops 1048576 | bytes 5242880 | tf_op jit(solution)/shard_map/convert_element_type | solution.py:122
  129.2 6.1 %collective-permute-done.8 = bf16[256,512]{1,0:T(8,128)(2,1)S(1)} collective-permute-done((bf16[256,512]{1,0:T(8,128)(2,1)S(1)}, bf16[256,512]{1,0:T(8,128)(2,1)S(1)}, u32[]{:S(2)}, u32[]{:S(2)}) %collective-permute-start.8) | collective-permute-done | bytes 262176 | tf_op jit(solution)/shard_map/ppermute | solution.py:127
  135.4 5.8 %collective-permute-done.9 = bf16[256,512]{1,0:T(8,128)(2,1)S(1)} collective-permute-done((bf16[256,512]{1,0:T(8,128)(2,1)S(1)}, bf16[256,512]{1,0:T(8,128)(2,1)S(1)}, u32[]{:S(2)}, u32[]{:S(2)}) %collective-permute-start.9) | collective-permute-done | bytes 262176 | tf_op jit(solution)/shard_map/ppermute | solution.py:127
  141.2 6.7 %fusion.14 = bf16[256,2048]{1,0:T(8,128)(2,1)} fusion(bf16[2048,2048]{1,0:T(8,128)(2,1)} %pad_maximum_fusion, bf16[256,2048]{1,0:T(8,128)(2,1)S(1)} %copy-done.1, bf16[256,512]{1,0:T(8,128)(2,1)S(1)} %collective-permute-done.9, bf16[256,512]{1,0:T(8,128)(2,1)S(1)} %collective-permute-done.8, bf16[256,512]{1,0:T(8,128)(2,1)S(1)} %collective-permute-done.7, ...), kind=kOutput, calls=%fused_computation.20 | convolution fusion | flops 2153250816 | bytes 11534336 | tf_op jit(solution)/shard_map/dot_general | solution.py:129
  (58 shorter events, 20.6 us)
Async XLA Ops:
  6.5 8.8 %copy-start.1 = (bf16[256,2048]{1,0:T(8,128)(2,1)S(1)}, bf16[256,2048]{1,0:T(8,128)(2,1)}, u32[]{:S(2)}) copy-start(bf16[256,2048]{1,0:T(8,128)(2,1)} %param.6) | copy-start | bytes 3145732
  6.5 73.5 %all-gather.2.cloned.1.call-start = ((), (), s32[]{:S(2)}) async-start(), calls=%async_computation | async-start | bytes 6684672 | tf_op jit(solution)/shard_map/all_gather | solution.py:67
  10.3 33.3 %collective-permute-start = (bf16[136,2048]{1,0:T(8,128)(2,1)S(1)}, bf16[136,2048]{1,0:T(8,128)(2,1)S(1)}, u32[]{:S(2)}, u32[]{:S(2)}) collective-permute-start(bf16[136,2048]{1,0:T(8,128)(2,1)S(1)} %slice.75), channel_id=1, source_target_pairs={{3,7},{7,11},{11,15},{19,23},{23,27},{27,31},{35,39},{39,43},{43,4... | collective-permute-start | bytes 1671176 | tf_op jit(solution)/shard_map/ppermute | solution.py:56
  11.0 37.3 %collective-permute-start.1 = (bf16[136,2048]{1,0:T(8,128)(2,1)S(1)}, bf16[136,2048]{1,0:T(8,128)(2,1)}, u32[]{:S(2)}, u32[]{:S(2)}) collective-permute-start(bf16[136,2048]{1,0:T(8,128)(2,1)S(1)} %slice.75), channel_id=1, source_target_pairs={{3,6},{7,10},{11,14},{19,22},{23,26},{27,30},{35,38},{39,42},{43,4... | collective-permute-start | bytes 1671176 | tf_op jit(solution)/shard_map/ppermute | solution.py:56
  12.4 35.8 %collective-permute-start.2 = (bf16[136,2048]{1,0:T(8,128)(2,1)S(1)}, bf16[136,2048]{1,0:T(8,128)(2,1)}, u32[]{:S(2)}, u32[]{:S(2)}) collective-permute-start(bf16[136,2048]{1,0:T(8,128)(2,1)S(1)} %slice.75), channel_id=1, source_target_pairs={{3,5},{7,9},{11,13},{19,21},{23,25},{27,29},{35,37},{39,41},{43,45... | collective-permute-start | bytes 1671176 | tf_op jit(solution)/shard_map/ppermute | solution.py:56
  13.9 34.4 %collective-permute-start.3 = (bf16[136,2048]{1,0:T(8,128)(2,1)S(1)}, bf16[136,2048]{1,0:T(8,128)(2,1)}, u32[]{:S(2)}, u32[]{:S(2)}) collective-permute-start(bf16[136,2048]{1,0:T(8,128)(2,1)S(1)} %slice.75), channel_id=1, source_target_pairs={{3,4},{7,8},{11,12},{19,20},{23,24},{27,28},{35,36},{39,40},{43,44... | collective-permute-start | bytes 1671176 | tf_op jit(solution)/shard_map/ppermute | solution.py:56
  15.4 28.6 %collective-permute-start.4 = (bf16[256,2048]{1,0:T(8,128)(2,1)S(1)}, bf16[256,2048]{1,0:T(8,128)(2,1)S(1)}, u32[]{:S(2)}, u32[]{:S(2)}) collective-permute-start(bf16[256,2048]{1,0:T(8,128)(2,1)S(1)} %copy-done.1), channel_id=1, source_target_pairs={{0,2},{1,3},{2,0},{3,1},{4,6},{5,7},{6,4},{7,5},{8,10},{9,11},{10,... | collective-permute-start | bytes 3145736 | tf_op jit(solution)/shard_map/ppermute | solution.py:43
  25.5 12.6 %copy-start.4 = (s32[1,4]{1,0:T(1,128)S(1)}, s32[1,4]{1,0:T(1,128)}, u32[]{:S(2)}) copy-start(s32[1,4]{1,0:T(1,128)} %param.7) | copy-start | bytes 52
  43.6 7.0 %collective-permute-start.6 = (bf16[256,2048]{1,0:T(8,128)(2,1)S(1)}, bf16[256,2048]{1,0:T(8,128)(2,1)S(1)}, u32[]{:S(2)}, u32[]{:S(2)}) collective-permute-start(bf16[256,2048]{1,0:T(8,128)(2,1)S(1)} %copy-done.1), channel_id=1, source_target_pairs={{0,1},{1,0},{2,3},{3,2},{4,5},{5,4},{6,7},{7,6},{8,9},{9,8},{10,11... | collective-permute-start | bytes 3145736 | tf_op jit(solution)/shard_map/ppermute | solution.py:41
  44.0 6.6 %collective-permute-start.5 = (bf16[256,2048]{1,0:T(8,128)(2,1)S(1)}, bf16[256,2048]{1,0:T(8,128)(2,1)S(1)}, u32[]{:S(2)}, u32[]{:S(2)}) collective-permute-start(bf16[256,2048]{1,0:T(8,128)(2,1)S(1)} %collective-permute-done.4), channel_id=1, source_target_pairs={{0,1},{1,0},{2,3},{3,2},{4,5},{5,4},{6,7},{7,6},{8,9},{9,8},{10,11... | collective-permute-start | bytes 3145736 | tf_op jit(solution)/shard_map/ppermute | solution.py:44
  101.9 2.9 %copy-start = (f32[1152,1536]{1,0:T(8,128)}, f32[1152,1536]{1,0:T(8,128)S(1)}, u32[]{:S(2)}) copy-start(f32[1152,1536]{1,0:T(8,128)S(1)} %multiply_add_fusion) | copy-start | bytes 21233668
  105.3 4.6 %copy-start.3 = (pred[8,128,128]{2,1,0:T(8,128)(4,1)S(1)}, pred[8,128,128]{2,1,0:T(8,128)(4,1)}, u32[]{:S(2)}) copy-start(pred[8,128,128]{2,1,0:T(8,128)(4,1)} %get-tuple-element.34) | copy-start | bytes 393220
  109.9 5.8 %copy-start.2 = (bf16[32,128,128]{2,1,0:T(8,128)(2,1)S(1)}, bf16[32,128,128]{2,1,0:T(8,128)(2,1)}, u32[]{:S(2)}) copy-start(bf16[32,128,128]{2,1,0:T(8,128)(2,1)} %copy.28) | copy-start | bytes 3145732
  126.7 2.5 %collective-permute-start.7 = (bf16[256,512]{1,0:T(8,128)(2,1)S(1)}, bf16[256,512]{1,0:T(8,128)(2,1)S(1)}, u32[]{:S(2)}, u32[]{:S(2)}) collective-permute-start(bf16[256,512]{1,0:T(8,128)(2,1)S(1)} %get-tuple-element.18), channel_id=1, source_target_pairs={{0,1},{1,0},{2,3},{3,2},{4,5},{5,4},{6,7},{7,6},{8,9},{9,8},{10,11... | collective-permute-start | bytes 786440 | tf_op jit(solution)/shard_map/ppermute | solution.py:127
  127.5 7.9 %collective-permute-start.8 = (bf16[256,512]{1,0:T(8,128)(2,1)S(1)}, bf16[256,512]{1,0:T(8,128)(2,1)S(1)}, u32[]{:S(2)}, u32[]{:S(2)}) collective-permute-start(bf16[256,512]{1,0:T(8,128)(2,1)S(1)} %get-tuple-element.17), channel_id=1, source_target_pairs={{0,2},{1,3},{2,0},{3,1},{4,6},{5,7},{6,4},{7,5},{8,10},{9,11},{10,... | collective-permute-start | bytes 786440 | tf_op jit(solution)/shard_map/ppermute | solution.py:127
  128.8 12.4 %collective-permute-start.9 = (bf16[256,512]{1,0:T(8,128)(2,1)S(1)}, bf16[256,512]{1,0:T(8,128)(2,1)S(1)}, u32[]{:S(2)}, u32[]{:S(2)}) collective-permute-start(bf16[256,512]{1,0:T(8,128)(2,1)S(1)} %get-tuple-element.16), channel_id=1, source_target_pairs={{0,3},{1,2},{2,1},{3,0},{4,7},{5,6},{6,5},{7,4},{8,11},{9,10},{10,... | collective-permute-start | bytes 786440 | tf_op jit(solution)/shard_map/ppermute | solution.py:127
Sparse Core Ops, SparseCore 0:
  9.8 70.1 all-gather.1
where the time goes:
time: 155 us
  matrix products  36 us (23%)
  waiting for transfers between devices  34.9 us (23%)
  other arithmetic  28.2 us (18%)
  local copies, waits for them, and re-layouts  25.5 us (16%)
  starting transfers between devices  16.5 us (11%)
  between operations  13.6 us (9%)
    all_gather x1, waiting for transfers between devices, local(): w_all = lax.all_gather(w_part, 'fsdp', axis=0, tiled=True)  22.7 us
    ppermute x3, waiting for transfers between devices, local(): got = send if d == 0 else lax.ppermute(send, 'seq', swaps[d - 1])  11.9 us
    dot_general x1, matrix products, local(): jnp.dot(ext_tokens, w_all.T, preferred_element_type=jnp.float32)  11.2 us
    add x1, other arithmetic, local(): featured + taps[tap_index] * jnp.where((pos_f >= tap_index)[:, None], shi...  10.7 us
    ppermute x1, starting transfers between devices, local(): fetched = lax.ppermute(tokens, 'seq', swaps[d - 1])  8.59 us
    unnamed x14, local copies, waits for them, and re-layouts  8.3 us
    dot_general x2, matrix products, tap_table(): jnp.einsum('ijt,tg->gij', one_hot, long_filter, preferred_element_type=jn...  7.92 us
    unnamed x4, other arithmetic  7.39 us
  transfers between devices with their start and end apart: 11, of which 4 were waited for; matrix products, arithmetic and copies ran while one was open for 22% of the time, Pallas kernels for 0%

commit v1 on v0

--- a/solution.py
+++ b/solution.py
@@ -64,7 +64,8 @@
     offset = member * part
     w_t = in_weight.T.reshape(in_weight.shape[1] // LANE, LANE, channels)
     w_part = lax.dynamic_slice_in_dim(w_t, offset, part, axis=1)
-    w_all = lax.all_gather(w_part, "fsdp", axis=0, tiled=True)
+    copies = jnp.concatenate([w_part] * lax.axis_size("fsdp"), axis=0)
+    w_all = lax.all_to_all(copies, "fsdp", 0, 0, tiled=True)
     own = n_lblk * part
     w_all = w_all.reshape(3 * own, channels)
     ow = out_weight.reshape(n_lblk, LANE, channels)

time: 155 us -> 213 us (1.37)
  the two profiles are of different devices: /device:TPU:1 before, /device:TPU:221 now
where the time goes in v1:
time: 213 us
  waiting for transfers between devices  92 us (43%)
  local copies, waits for them, and re-layouts  38.3 us (18%)
  matrix products  36 us (17%)
  other arithmetic  28.5 us (13%)
  starting transfers between devices  17.4 us (8%)
    all_to_all x1, waiting for transfers between devices, local(): w_all = lax.all_to_all(copies, 'fsdp', 0, 0, tiled=True)  80.1 us
    unnamed x31, local copies, waits for them, and re-layouts  18.3 us
    ppermute x3, waiting for transfers between devices, local(): got = send if d == 0 else lax.ppermute(send, 'seq', swaps[d - 1])  11.9 us
    dot_general x1, matrix products, local(): jnp.dot(ext_tokens, w_all.T, preferred_element_type=jnp.float32)  11.2 us
    add x1, other arithmetic, local(): featured + taps[tap_index] * jnp.where((pos_f >= tap_index)[:, None], shi...  10.7 us
    dot_general x2, matrix products, tap_table(): jnp.einsum('ijt,tg->gij', one_hot, long_filter, preferred_element_type=jn...  7.91 us
    unnamed x4, other arithmetic  7.36 us
    all_to_all x1, starting transfers between devices, local(): w_all = lax.all_to_all(copies, 'fsdp', 0, 0, tiled=True)  6.68 us
  transfers between devices with their start and end apart: 11, of which 3 were waited for; matrix products, arithmetic and copies ran while one was open for 21% of the time, Pallas kernels for 0%

profile of v1, /device:TPU:221, one launch (start us, length us, event | category | flops | bytes accessed | tf_op | source)
XLA Modules:
  0.0 212.6 jit_solution(9981759015373712816)
XLA Ops:
  0.0 1.9 slice.75
  8.4 1.7 copy.17
  22.6 6.7 %all-to-all-start = ((bf16[48,32,2048]{2,1,0:T(8,128)(2,1)}), bf16[48,32,2048]{2,1,0:T(8,128)(2,1)}, u32[]{:S(2)}, u32[]{:S(2)}) async-start(bf16[48,32,2048]{2,1,0:T(8,128)(2,1)} %constant_dynamic-update-slice_fusion), calls=%async_computation | async-start | bytes 12582912 | tf_op jit(solution)/shard_map/all_to_all | solution.py:68
  30.4 4.0 %fusion.20 = bf16[32,128,128]{2,0,1:T(8,128)(2,1)S(1)} fusion(bf16[128,32,1]{0,1,2:T(8,128)(2,1)S(1)} %bitcast.92, s32[128,128]{1,0:T(8,128)S(1)} %get-tuple-element.35), kind=kOutput, calls=%fused_computation.28 | convolution fusion | flops 136839168 | bytes 1122304 | tf_op jit(solution)/shard_map/ijt,tg->gij/dot_general | solution.py:22
  35.8 3.9 %fusion.21 = bf16[32,128,128]{2,0,1:T(8,128)(2,1)S(1)} fusion(bf16[128,32,1]{0,1,2:T(8,128)(2,1)S(1)} %bitcast.93, s32[128,128]{1,0:T(8,128)S(1)} %get-tuple-element.36), kind=kOutput, calls=%fused_computation.29 | convolution fusion | flops 136839168 | bytes 1122304 | tf_op jit(solution)/shard_map/ijt,tg->gij/dot_general | solution.py:22
  41.6 4.4 %constant_dynamic-slice_fusion.11 = (bf16[16,32,2048]{2,1,0:T(8,128)(2,1)S(1)}, bf16[16,32,2048]{2,1,0:T(8,128)(2,1)S(1)}, bf16[16,32,2048]{2,1,0:T(8,128)(2,1)S(1)}, bf16[16,32,2048]{2,1,0:T(8,128)(2,1)S(1)}) fusion(bf16[16,128,2048]{2,1,0:T(8,128)(2,1)} %bitcast.81, s32[]{:T(128)S(6)} %select_n.178, s32[]{:T(128)S(6)} %select_n.215, s32[]{:T(128)S(6)} %select_n.214, ...), kind=kLoop, calls=%fused_computation.89 | loop fusion | bytes 16777232 | tf_op jit(solution)/shard_map/dynamic_slice | solution.py:76
  47.1 4.1 %pad_maximum_fusion = bf16[2048,2048]{1,0:T(8,128)(2,1)} fusion(bf16[512,2048]{1,0:T(8,128)(2,1)S(1)} %bitcast.85, bf16[512,2048]{1,0:T(8,128)(2,1)S(1)} %bitcast.86, bf16[512,2048]{1,0:T(8,128)(2,1)S(1)} %bitcast.87, bf16[512,2048]{1,0:T(8,128)(2,1)S(1)} %bitcast.84), kind=kLoop, calls=%fused_computation | loop fusion | flops 33554432 | bytes 16777216 | tf_op jit(solution)/shard_map/concatenate | solution.py:78
  51.2 2.3 %select_dynamic-update-slice_fusion.4 = bf16[1160,2048]{1,0:T(8,128)(2,1)} fusion(bf16[136,2048]{1,0:T(8,128)(2,1)S(1)} %collective-permute-done, bf16[136,2048]{1,0:T(8,128)(2,1)} %collective-permute-done.1, bf16[136,2048]{1,0:T(8,128)(2,1)} %collective-permute-done.2, bf16[136,2048]{1,0:T(8,128)(2,1)} %collective-permute-done.3, pred[]{:T(512)S(6)} %eq.79, ...), kind=kLoop, calls=%fused_computation.44 | loop fusion | flops 1114111 | bytes 2785284
  53.5 1.7 select_dynamic-update-slice_fusion.3
  58.6 1.7 select_dynamic-update-slice_fusion
  60.3 80.1 %all-to-all-done = bf16[48,32,2048]{2,1,0:T(8,128)(2,1)} async-done(((bf16[48,32,2048]{2,1,0:T(8,128)(2,1)}), bf16[48,32,2048]{2,1,0:T(8,128)(2,1)}, u32[]{:S(2)}, u32[]{:S(2)}) %all-to-all-start) | async-done | bytes 6291488 | tf_op jit(solution)/shard_map/all_to_all | solution.py:68
  140.4 11.2 %convolution_convert_fusion = bf16[1160,1536]{1,0:T(8,128)(2,1)S(1)} fusion(bf16[1160,2048]{1,0:T(8,128)(2,1)} %select_dynamic-update-slice_fusion, bf16[1536,2048]{1,0:T(8,128)(2,1)} %bitcast.8), kind=kOutput, calls=%fused_computation.11 | convolution fusion | flops 7299870720 | bytes 14606336 | tf_op jit(solution)/shard_map/dot_general | solution.py:80
  151.6 10.7 %multiply_add_fusion = f32[1152,1536]{1,0:T(8,128)S(1)} fusion(bf16[1160,1536]{1,0:T(8,128)(2,1)S(1)} %convolution_convert_fusion, f32[1536]{0:T(1024)S(1)} %mul.115, f32[1536]{0:T(1024)S(1)} %mul.112, f32[1536]{0:T(1024)S(1)} %mul.109, f32[1536]{0:T(1024)S(1)} %mul.106, f32[1536]{0:T(1024)S(1)} %mul.103, f32[1536]{0:T(1024)S(1)} %mul.100, ...), kind=kLoop, calls=%fused_computation.12 | loop fusion | flops 47775744 | bytes 31901568 | tf_op jit(solution)/shard_map/add | solution.py:91
  162.3 2.9 %copy-done = f32[1152,1536]{1,0:T(8,128)} copy-done((f32[1152,1536]{1,0:T(8,128)}, f32[1152,1536]{1,0:T(8,128)S(1)}, u32[]{:S(2)}) %copy-start) | copy-done | bytes 7077912
  170.0 2.3 %fusion.36 = (bf16[32,16,8,128]{3,2,1,0:T(8,128)(2,1)S(1)}, bf16[32,16,8,128]{3,2,1,0:T(8,128)(2,1)S(1)}) fusion(bf16[32,16,9,128]{3,2,1,0:T(8,128)(2,1)} %reshape.154), kind=kLoop, calls=%fused_computation.98 | loop fusion | bytes 4194304 | tf_op jit(solution)/shard_map/slice | solution.py:117
  172.3 5.8 %fusion = f32[32,8,128,16]{2,3,1,0:T(8,128)S(1)} fusion(pred[8,128,128]{2,1,0:T(8,128)(4,1)S(1)} %get-tuple-element.34, bf16[32,128,128]{2,1,0:T(8,128)(2,1)} %copy.22, bf16[32,16,8,128]{3,2,1,0:T(8,128)(2,1)S(1)} %get-tuple-element.14), kind=kOutput, calls=%fused_computation.1 | convolution fusion | flops 138412032 | bytes 4325376 | tf_op jit(solution)/shard_map/gcbj,bgij->gcbi/dot_general | solution.py:119
  178.1 4.5 %add_bitcast_fusion = f32[32,16,8,128]{3,1,2,0:T(8,128)S(1)} fusion(f32[32,8,128,16]{2,3,1,0:T(8,128)S(1)} %fusion, pred[8,128,128]{2,1,0:T(8,128)(4,1)S(1)} %get-tuple-element.33, bf16[32,128,128]{2,1,0:T(8,128)(2,1)S(1)} %copy-done.2, bf16[32,16,8,128]{3,2,1,0:T(8,128)(2,1)S(1)} %get-tuple-element.13), kind=kOutput, calls=%fused_computation.27 | convolution fusion | flops 138936320 | bytes 6422528 | tf_op jit(solution)/shard_map/gcbj,bgij->gcbi/dot_general | solution.py:116
  183.4 1.8 copy.35
  185.2 2.9 %copy.25 = f32[512,1024]{0,1:T(8,128)} copy(f32[512,1024]{1,0:T(8,128)} %bitcast.83) | data formatting | bytes 4194304 | tf_op jit(solution)/shard_map/reshape | solution.py:122
  188.1 2.6 %fusion.17 = bf16[512,1024]{0,1:T(8,128)(2,1)S(1)} fusion(f32[512,1024]{0,1:T(8,128)} %copy.25, f32[1152,1536]{1,0:T(8,128)} %copy-done), kind=kLoop, calls=%fused_computation.26 | loop fusion | flops 1048576 | bytes 5242880 | tf_op jit(solution)/shard_map/convert_element_type | solution.py:123
  192.2 1.7 collective-permute-start.9
  193.9 6.1 %collective-permute-done.8 = bf16[256,512]{1,0:T(8,128)(2,1)S(1)} collective-permute-done((bf16[256,512]{1,0:T(8,128)(2,1)S(1)}, bf16[256,512]{1,0:T(8,128)(2,1)S(1)}, u32[]{:S(2)}, u32[]{:S(2)}) %collective-permute-start.8) | collective-permute-done | bytes 262176 | tf_op jit(solution)/shard_map/ppermute | solution.py:128
  200.1 5.8 %collective-permute-done.9 = bf16[256,512]{1,0:T(8,128)(2,1)S(1)} collective-permute-done((bf16[256,512]{1,0:T(8,128)(2,1)S(1)}, bf16[256,512]{1,0:T(8,128)(2,1)S(1)}, u32[]{:S(2)}, u32[]{:S(2)}) %collective-permute-start.9) | collective-permute-done | bytes 262176 | tf_op jit(solution)/shard_map/ppermute | solution.py:128
  205.9 6.7 %fusion.14 = bf16[256,2048]{1,0:T(8,128)(2,1)} fusion(bf16[2048,2048]{1,0:T(8,128)(2,1)} %pad_maximum_fusion, bf16[256,2048]{1,0:T(8,128)(2,1)S(1)} %copy-done.1, bf16[256,512]{1,0:T(8,128)(2,1)S(1)} %collective-permute-done.9, bf16[256,512]{1,0:T(8,128)(2,1)S(1)} %collective-permute-done.8, bf16[256,512]{1,0:T(8,128)(2,1)S(1)} %collective-permute-done.7, ...), kind=kOutput, calls=%fused_computation.20 | convolution fusion | flops 2153250816 | bytes 11534336 | tf_op jit(solution)/shard_map/dot_general | solution.py:130
  (74 shorter events, 34.9 us)
Async XLA Ops:
  1.9 44.1 %collective-permute-start = (bf16[136,2048]{1,0:T(8,128)(2,1)}, bf16[136,2048]{1,0:T(8,128)(2,1)S(1)}, u32[]{:S(2)}, u32[]{:S(2)}) collective-permute-start(bf16[136,2048]{1,0:T(8,128)(2,1)} %slice.75), channel_id=1, source_target_pairs={{3,7},{7,11},{11,15},{19,23},{23,27},{27,31},{35,39},{39,43},{43,4... | collective-permute-start | bytes 1671176 | tf_op jit(solution)/shard_map/ppermute | solution.py:56
  2.6 48.6 %collective-permute-start.1 = (bf16[136,2048]{1,0:T(8,128)(2,1)}, bf16[136,2048]{1,0:T(8,128)(2,1)}, u32[]{:S(2)}, u32[]{:S(2)}) collective-permute-start(bf16[136,2048]{1,0:T(8,128)(2,1)} %slice.75), channel_id=1, source_target_pairs={{3,6},{7,10},{11,14},{19,22},{23,26},{27,30},{35,38},{39,42},{43,4... | collective-permute-start | bytes 1671176 | tf_op jit(solution)/shard_map/ppermute | solution.py:56
  4.1 47.1 %collective-permute-start.2 = (bf16[136,2048]{1,0:T(8,128)(2,1)}, bf16[136,2048]{1,0:T(8,128)(2,1)}, u32[]{:S(2)}, u32[]{:S(2)}) collective-permute-start(bf16[136,2048]{1,0:T(8,128)(2,1)} %slice.75), channel_id=1, source_target_pairs={{3,5},{7,9},{11,13},{19,21},{23,25},{27,29},{35,37},{39,41},{43,45... | collective-permute-start | bytes 1671176 | tf_op jit(solution)/shard_map/ppermute | solution.py:56
  5.4 45.8 %collective-permute-start.3 = (bf16[136,2048]{1,0:T(8,128)(2,1)}, bf16[136,2048]{1,0:T(8,128)(2,1)}, u32[]{:S(2)}, u32[]{:S(2)}) collective-permute-start(bf16[136,2048]{1,0:T(8,128)(2,1)} %slice.75), channel_id=1, source_target_pairs={{3,4},{7,8},{11,12},{19,20},{23,24},{27,28},{35,36},{39,40},{43,44... | collective-permute-start | bytes 1671176 | tf_op jit(solution)/shard_map/ppermute | solution.py:56
  6.9 40.0 %collective-permute-start.4 = (bf16[256,2048]{1,0:T(8,128)(2,1)}, bf16[256,2048]{1,0:T(8,128)(2,1)S(1)}, u32[]{:S(2)}, u32[]{:S(2)}) collective-permute-start(bf16[256,2048]{1,0:T(8,128)(2,1)} %param.6), channel_id=1, source_target_pairs={{0,2},{1,3},{2,0},{3,1},{4,6},{5,7},{6,4},{7,5},{8,10},{9,11},{10,... | collective-permute-start | bytes 3145736 | tf_op jit(solution)/shard_map/ppermute | solution.py:43
  22.6 6.7 %copy-start.3 = (f32[7,6144]{1,0:T(8,128)S(1)}, f32[7,6144]{1,0:T(8,128)}, u32[]{:S(2)}) copy-start(f32[7,6144]{1,0:T(8,128)} %param.9) | copy-start | bytes 516100
  22.6 7.1 %copy-start.4 = (bf16[128,128]{1,0:T(8,128)(2,1)S(1)}, bf16[128,128]{1,0:T(8,128)(2,1)}, u32[]{:S(2)}) copy-start(bf16[128,128]{1,0:T(8,128)(2,1)} %param.10) | copy-start | bytes 98308
  22.6 7.7 %copy-start.5 = (s32[1,4]{1,0:T(1,128)S(1)}, s32[1,4]{1,0:T(1,128)}, u32[]{:S(2)}) copy-start(s32[1,4]{1,0:T(1,128)} %param.7) | copy-start | bytes 52
  22.6 117.8 %all-to-all-start = ((bf16[48,32,2048]{2,1,0:T(8,128)(2,1)}), bf16[48,32,2048]{2,1,0:T(8,128)(2,1)}, u32[]{:S(2)}, u32[]{:S(2)}) async-start(bf16[48,32,2048]{2,1,0:T(8,128)(2,1)} %constant_dynamic-update-slice_fusion), calls=%async_computation | async-start | bytes 12582912 | tf_op jit(solution)/shard_map/all_to_all | solution.py:68
  41.6 4.4 %copy-start.1 = (bf16[256,2048]{1,0:T(8,128)(2,1)S(1)}, bf16[256,2048]{1,0:T(8,128)(2,1)}, u32[]{:S(2)}) copy-start(bf16[256,2048]{1,0:T(8,128)(2,1)} %param.6) | copy-start | bytes 3145732
  46.0 7.5 %collective-permute-start.6 = (bf16[256,2048]{1,0:T(8,128)(2,1)S(1)}, bf16[256,2048]{1,0:T(8,128)(2,1)S(1)}, u32[]{:S(2)}, u32[]{:S(2)}) collective-permute-start(bf16[256,2048]{1,0:T(8,128)(2,1)S(1)} %copy-done.1), channel_id=1, source_target_pairs={{0,1},{1,0},{2,3},{3,2},{4,5},{5,4},{6,7},{7,6},{8,9},{9,8},{10,11... | collective-permute-start | bytes 3145736 | tf_op jit(solution)/shard_map/ppermute | solution.py:41
  46.9 6.7 %collective-permute-start.5 = (bf16[256,2048]{1,0:T(8,128)(2,1)S(1)}, bf16[256,2048]{1,0:T(8,128)(2,1)S(1)}, u32[]{:S(2)}, u32[]{:S(2)}) collective-permute-start(bf16[256,2048]{1,0:T(8,128)(2,1)S(1)} %collective-permute-done.4), channel_id=1, source_target_pairs={{0,1},{1,0},{2,3},{3,2},{4,5},{5,4},{6,7},{7,6},{8,9},{9,8},{10,11... | collective-permute-start | bytes 3145736 | tf_op jit(solution)/shard_map/ppermute | solution.py:44
  162.3 2.9 %copy-start = (f32[1152,1536]{1,0:T(8,128)}, f32[1152,1536]{1,0:T(8,128)S(1)}, u32[]{:S(2)}) copy-start(f32[1152,1536]{1,0:T(8,128)S(1)} %multiply_add_fusion) | copy-start | bytes 21233668
  172.3 5.8 %copy-start.2 = (bf16[32,128,128]{2,1,0:T(8,128)(2,1)S(1)}, bf16[32,128,128]{2,1,0:T(8,128)(2,1)}, u32[]{:S(2)}) copy-start(bf16[32,128,128]{2,1,0:T(8,128)(2,1)} %copy.19) | copy-start | bytes 3145732
  190.8 3.2 %collective-permute-start.7 = (bf16[256,512]{1,0:T(8,128)(2,1)S(1)}, bf16[256,512]{1,0:T(8,128)(2,1)S(1)}, u32[]{:S(2)}, u32[]{:S(2)}) collective-permute-start(bf16[256,512]{1,0:T(8,128)(2,1)S(1)} %get-tuple-element.18), channel_id=1, source_target_pairs={{0,1},{1,0},{2,3},{3,2},{4,5},{5,4},{6,7},{7,6},{8,9},{9,8},{10,11... | collective-permute-start | bytes 786440 | tf_op jit(solution)/shard_map/ppermute | solution.py:128
  192.2 7.9 %collective-permute-start.8 = (bf16[256,512]{1,0:T(8,128)(2,1)S(1)}, bf16[256,512]{1,0:T(8,128)(2,1)S(1)}, u32[]{:S(2)}, u32[]{:S(2)}) collective-permute-start(bf16[256,512]{1,0:T(8,128)(2,1)S(1)} %get-tuple-element.17), channel_id=1, source_target_pairs={{0,2},{1,3},{2,0},{3,1},{4,6},{5,7},{6,4},{7,5},{8,10},{9,11},{10,... | collective-permute-start | bytes 786440 | tf_op jit(solution)/shard_map/ppermute | solution.py:128
  192.2 13.7 %collective-permute-start.9 = (bf16[256,512]{1,0:T(8,128)(2,1)S(1)}, bf16[256,512]{1,0:T(8,128)(2,1)S(1)}, u32[]{:S(2)}, u32[]{:S(2)}) collective-permute-start(bf16[256,512]{1,0:T(8,128)(2,1)S(1)} %get-tuple-element.16), channel_id=1, source_target_pairs={{0,3},{1,2},{2,1},{3,0},{4,7},{5,6},{6,5},{7,4},{8,11},{9,10},{10,... | collective-permute-start | bytes 786440 | tf_op jit(solution)/shard_map/ppermute | solution.py:128
